TPU v7x, 256 devices: a whole 4x4x8 slice. The times are simulated.
256 devices in a mesh: tm: 64 (over z, y, core), ingest: 4 (over x).
Axes of the slice: x: 4, y: 4, z: 8, core: 2. Of those that a mesh axis runs over, the one named last changes fastest.
Arguments:
- trans: float32 [512, 384, 384], P('tm')
- gain: float32 [512, 384, 192], P('tm', None, 'ingest'), may hold values from -0.0048828125 to 0.0048828125
- prior_mean: float32 [384], replicated, may hold values from -8 to 8
- obs_basis: bfloat16 [131072, 192], P(('tm', 'ingest')), may hold values from -6 to 6
- obs_value: float32 [131072], P(('tm', 'ingest')), may hold values from -6 to 6
- measurement_within_tile: int32 [131072], P(('tm', 'ingest')), may hold values from 0 to 7
- observed_row_count: int32 [256, 64], P(('tm', 'ingest')), may hold values from 1 to 8, as said below
Outputs:
- filtered: float32 [512, 384], P('tm')
Inputs may be any that keep to these rules, and one draw needn't show every extreme that they name: `observed_row_count`: rows of a group at positions from its count on are not live; every device's row of counts has one group of 8 live rows.
All inputs are finite; a program needn't handle non-finite values.
Results may differ from a plain program's by a relative error of at most 0.0023.
Values may be sent and summed in bfloat16 or wider, within the bound.
No kernel may reach another device: no remote copies, remote signals or barrier semaphores. Data moves between devices by JAX's collectives and lax.ppermute only.
A program may use at most 128 MiB of HBM per device.

v0:
```python
import jax
import jax.numpy as jnp
from jax import lax
from jax.sharding import PartitionSpec as P


def passed_along(block, axis, distance):
    devices = range(lax.axis_size(axis))
    route = [(i - distance, i) for i in devices if i - distance in devices]
    return lax.ppermute(block, axis, route)


def on_device(
    trans, gain, prior_mean, obs_basis, obs_value, measurement_within_tile, observed_row_count
):
    exact = lax.Precision.HIGHEST
    tm_count = lax.axis_size("tm")
    in_count = lax.axis_size("ingest")
    steps_here = trans.shape[0]
    state_width = trans.shape[1]
    basis_count = obs_basis.shape[1]
    piece_width = basis_count // in_count
    group_rows = obs_basis.shape[0] // tm_count
    weighted = (obs_basis.astype(jnp.float32) * obs_value[:, None]).astype(jnp.bfloat16)
    pieces = weighted.reshape(tm_count, group_rows, in_count, piece_width)
    pieces = pieces.transpose(0, 2, 1, 3).reshape(tm_count * in_count, group_rows * piece_width)
    is_valid = lax.broadcasted_iota(
        jnp.int32, (tm_count, group_rows), 1
    ) < observed_row_count.reshape(tm_count, 1)
    marked = jnp.where(is_valid, measurement_within_tile.reshape(tm_count, group_rows), -1)
    marks = jnp.broadcast_to(
        marked.astype(jnp.bfloat16)[:, None, :], (tm_count, in_count, group_rows)
    ).reshape(tm_count * in_count, group_rows)
    sent = jnp.concatenate([pieces, marks], axis=1)
    got = lax.all_to_all(sent, ("tm", "ingest"), split_axis=0, concat_axis=0, tiled=True)
    got_rows = got[:, : group_rows * piece_width].reshape(-1, piece_width)
    got_marks = got[:, group_rows * piece_width :].reshape(-1).astype(jnp.int32)
    step_ids = lax.broadcasted_iota(jnp.int32, (1, steps_here), 1)
    onehot = (got_marks[:, None] == step_ids).astype(jnp.bfloat16)
    drive_piece = jnp.einsum("rl,rq->lq", onehot, got_rows, preferred_element_type=jnp.float32)
    partial_force = jnp.einsum("lsq,lq->ls", gain, drive_piece, precision=exact)
    forcing = lax.psum(partial_force, "ingest")

    def compose(prefix, step_map):
        prefix = jnp.dot(step_map, prefix, precision=exact)
        return (prefix, prefix)

    _, prefix_maps = lax.scan(compose, jnp.eye(state_width, dtype=jnp.float32), trans)

    def advance(offset, inputs):
        step_map, step_force = inputs
        offset = jnp.dot(step_map, offset, precision=exact) + step_force
        return (offset, offset)

    _, offsets = lax.scan(advance, jnp.zeros((state_width,), jnp.float32), (trans, forcing))
    tm_index = lax.axis_index("tm")
    is_first = tm_index == 0
    slab_map = prefix_maps[-1]
    acc_vec = jnp.where(
        is_first, jnp.dot(slab_map, prior_mean, precision=exact) + offsets[-1], offsets[-1]
    )
    acc_map = jnp.where(is_first, jnp.zeros_like(slab_map), slab_map)
    distance = 1
    while distance < tm_count:
        got_vec = passed_along(acc_vec, "tm", distance)
        last = distance * 2 >= tm_count
        if not last:
            got_map = passed_along(acc_map, "tm", distance)
        acc_vec = jnp.dot(acc_map, got_vec, precision=exact) + acc_vec
        if not last:
            acc_map = jnp.dot(acc_map, got_map, precision=exact)
        distance *= 2
    entering = jnp.where(is_first, prior_mean, passed_along(acc_vec, "tm", 1))
    filtered = jnp.einsum("lsq,q->ls", prefix_maps, entering, precision=exact) + offsets
    return filtered


def solution(mesh):
    return jax.shard_map(
        on_device,
        mesh=mesh,
        in_specs=(
            P("tm", None, None),
            P("tm", None, "ingest"),
            P(),
            P(("tm", "ingest"), None),
            P(("tm", "ingest")),
            P(("tm", "ingest")),
            P(("tm", "ingest"), None),
        ),
        out_specs=P("tm", None),
        check_vma=False,
    )
```

profile of v0, /device:TPU:128, one launch (start us, length us, event | category | flops | bytes accessed | tf_op | source)
XLA Modules:
  0.0 224.0 jit_solution(79529686420630875)
XLA Ops:
  0.1 25.7 %while.25 = (s32[]{:T(128)}, f32[384,384]{1,0:T(8,128)S(1)}, f32[8,384,384]{2,1,0:T(8,128)}, f32[8,384,384]{2,1,0:T(8,128)}, s32[]{:T(128)}) while((s32[]{:T(128)}, f32[384,384]{1,0:T(8,128)S(1)}, f32[8,384,384]{2,1,0:T(8,128)}, f32[8,384,384]{2,1,0:T(8,128)}, s32[]{:T(128)}) %tuple.41), condition=%wide.region_1.2_spmd, body=%wide.region_0.1_spmd.sunk | while | flops 679477248 | bytes 3540037 | solution.py:48
  0.2 3.2 %bitcast_dynamic-update-slice_fusion.2 = (f32[8,384,384]{2,1,0:T(8,128)}, f32[384,384]{1,0:T(8,128)S(1)}) fusion(f32[8,384,384]{2,1,0:T(8,128)} %get-tuple-element.182, s32[]{:T(128)S(6)} %copy.40, f32[384,384]{1,0:T(8,128)S(1)} %copy.47, f32[8,384,384]{2,1,0:T(8,128)} %get-tuple-element.188), kind=kOutput, calls=%fused_computation.clone.1 | convolution fusion | flops 679477248 | bytes 2360320 | tf_op jit(solution)/shard_map/while/body/eval_jaxpr/dot_general | solution.py:45
  3.4 3.1 %bitcast_dynamic-update-slice_fusion.2 = (f32[8,384,384]{2,1,0:T(8,128)}, f32[384,384]{1,0:T(8,128)S(1)}) fusion(f32[8,384,384]{2,1,0:T(8,128)} %get-tuple-element.182, s32[]{:T(128)S(6)} %copy.40, f32[384,384]{1,0:T(8,128)S(1)} %copy.47, f32[8,384,384]{2,1,0:T(8,128)} %get-tuple-element.188), kind=kOutput, calls=%fused_computation.clone.1 | convolution fusion | flops 679477248 | bytes 2360320 | tf_op jit(solution)/shard_map/while/body/eval_jaxpr/dot_general | solution.py:45
  6.6 3.2 %bitcast_dynamic-update-slice_fusion.2 = (f32[8,384,384]{2,1,0:T(8,128)}, f32[384,384]{1,0:T(8,128)S(1)}) fusion(f32[8,384,384]{2,1,0:T(8,128)} %get-tuple-element.182, s32[]{:T(128)S(6)} %copy.40, f32[384,384]{1,0:T(8,128)S(1)} %copy.47, f32[8,384,384]{2,1,0:T(8,128)} %get-tuple-element.188), kind=kOutput, calls=%fused_computation.clone.1 | convolution fusion | flops 679477248 | bytes 2360320 | tf_op jit(solution)/shard_map/while/body/eval_jaxpr/dot_general | solution.py:45
  9.8 3.2 %bitcast_dynamic-update-slice_fusion.2 = (f32[8,384,384]{2,1,0:T(8,128)}, f32[384,384]{1,0:T(8,128)S(1)}) fusion(f32[8,384,384]{2,1,0:T(8,128)} %get-tuple-element.182, s32[]{:T(128)S(6)} %copy.40, f32[384,384]{1,0:T(8,128)S(1)} %copy.47, f32[8,384,384]{2,1,0:T(8,128)} %get-tuple-element.188), kind=kOutput, calls=%fused_computation.clone.1 | convolution fusion | flops 679477248 | bytes 2360320 | tf_op jit(solution)/shard_map/while/body/eval_jaxpr/dot_general | solution.py:45
  13.0 3.2 %bitcast_dynamic-update-slice_fusion.2 = (f32[8,384,384]{2,1,0:T(8,128)}, f32[384,384]{1,0:T(8,128)S(1)}) fusion(f32[8,384,384]{2,1,0:T(8,128)} %get-tuple-element.182, s32[]{:T(128)S(6)} %copy.40, f32[384,384]{1,0:T(8,128)S(1)} %copy.47, f32[8,384,384]{2,1,0:T(8,128)} %get-tuple-element.188), kind=kOutput, calls=%fused_computation.clone.1 | convolution fusion | flops 679477248 | bytes 2360320 | tf_op jit(solution)/shard_map/while/body/eval_jaxpr/dot_general | solution.py:45
  16.2 3.1 %bitcast_dynamic-update-slice_fusion.2 = (f32[8,384,384]{2,1,0:T(8,128)}, f32[384,384]{1,0:T(8,128)S(1)}) fusion(f32[8,384,384]{2,1,0:T(8,128)} %get-tuple-element.182, s32[]{:T(128)S(6)} %copy.40, f32[384,384]{1,0:T(8,128)S(1)} %copy.47, f32[8,384,384]{2,1,0:T(8,128)} %get-tuple-element.188), kind=kOutput, calls=%fused_computation.clone.1 | convolution fusion | flops 679477248 | bytes 2360320 | tf_op jit(solution)/shard_map/while/body/eval_jaxpr/dot_general | solution.py:45
  19.4 3.1 %bitcast_dynamic-update-slice_fusion.2 = (f32[8,384,384]{2,1,0:T(8,128)}, f32[384,384]{1,0:T(8,128)S(1)}) fusion(f32[8,384,384]{2,1,0:T(8,128)} %get-tuple-element.182, s32[]{:T(128)S(6)} %copy.40, f32[384,384]{1,0:T(8,128)S(1)} %copy.47, f32[8,384,384]{2,1,0:T(8,128)} %get-tuple-element.188), kind=kOutput, calls=%fused_computation.clone.1 | convolution fusion | flops 679477248 | bytes 2360320 | tf_op jit(solution)/shard_map/while/body/eval_jaxpr/dot_general | solution.py:45
  22.6 3.1 %bitcast_dynamic-update-slice_fusion.2 = (f32[8,384,384]{2,1,0:T(8,128)}, f32[384,384]{1,0:T(8,128)S(1)}) fusion(f32[8,384,384]{2,1,0:T(8,128)} %get-tuple-element.182, s32[]{:T(128)S(6)} %copy.40, f32[384,384]{1,0:T(8,128)S(1)} %copy.47, f32[8,384,384]{2,1,0:T(8,128)} %get-tuple-element.188), kind=kOutput, calls=%fused_computation.clone.1 | convolution fusion | flops 679477248 | bytes 2360320 | tf_op jit(solution)/shard_map/while/body/eval_jaxpr/dot_general | solution.py:45
  25.8 1.1 bitcast_select_fusion
  26.9 1.9 collective-permute-start
  29.0 12.4 %collective-permute-done = f32[384,384]{1,0:T(8,128)S(1)} collective-permute-done((f32[384,384]{1,0:T(8,128)S(1)}, f32[384,384]{1,0:T(8,128)S(1)}, u32[]{:S(2)}, u32[]{:S(2)}) %collective-permute-start) | collective-permute-done | bytes 589856 | tf_op jit(solution)/shard_map/ppermute | solution.py:10
  41.4 1.3 fusion.12
  42.7 1.9 collective-permute-start.1
  46.2 0.8 reduce.20
  47.0 0.9 reshape.87
  47.8 13.9 %all-to-all-start = ((bf16[256,2,196]{2,1,0:T(2,128)(2,1)}), bf16[256,2,196]{2,1,0:T(2,128)(2,1)S(1)}, u32[]{:S(2)}, u32[]{:S(2)}) async-start(bf16[256,2,196]{2,1,0:T(2,128)(2,1)} %reshape.87), calls=%async_computation | async-start | bytes 524288 | tf_op jit(solution)/shard_map/all_to_all | solution.py:35
  61.8 1.7 convolution_reduce_fusion.7
  63.5 8.7 %all-to-all-done = bf16[256,2,196]{2,1,0:T(2,128)(2,1)S(1)} async-done(((bf16[256,2,196]{2,1,0:T(2,128)(2,1)}), bf16[256,2,196]{2,1,0:T(2,128)(2,1)S(1)}, u32[]{:S(2)}, u32[]{:S(2)}) %all-to-all-start) | async-done | bytes 200736 | tf_op jit(solution)/shard_map/all_to_all | solution.py:35
  72.9 1.3 fusion.13
  74.2 3.3 %collective-permute-start.2 = (f32[384,384]{1,0:T(8,128)S(1)}, f32[384,384]{1,0:T(8,128)S(1)}, u32[]{:S(2)}, u32[]{:S(2)}) collective-permute-start(f32[384,384]{1,0:T(8,128)S(1)} %fusion.13), channel_id=1, source_target_pairs={{0,16},{4,20},{8,24},{12,28},{16,32},{20,36},{24,40},{28,44},{32,4... | collective-permute-start | bytes 1769480 | tf_op jit(solution)/shard_map/ppermute | solution.py:10
  77.7 1.3 reshape.55
  79.2 1.7 fusion.7
  81.4 15.5 %psum.7 = f32[8,384]{1,0:T(8,128)} all-reduce(f32[8,384]{1,0:T(8,128)S(1)} %bitcast.74), channel_id=1, replica_groups=mesh['tm'=64,'ingest'=4] {'ingest'}, use_global_device_ids=true, to_apply=%region_2.3 | all-reduce | flops 3072 | bytes 24576 | tf_op jit(solution)/shard_map/psum | solution.py:42
  96.9 1.3 fusion.14
  98.2 2.6 %collective-permute-start.3 = (f32[384,384]{1,0:T(8,128)S(1)}, f32[384,384]{1,0:T(8,128)S(1)}, u32[]{:S(2)}, u32[]{:S(2)}) collective-permute-start(f32[384,384]{1,0:T(8,128)S(1)} %fusion.14), channel_id=1, source_target_pairs={{0,32},{4,36},{8,40},{12,44},{16,48},{20,52},{24,56},{28,60},{32,6... | collective-permute-start | bytes 1769480 | tf_op jit(solution)/shard_map/ppermute | solution.py:10
  100.7 30.5 %while.26 = (s32[]{:T(128)}, f32[384]{0:T(512)S(1)}, f32[8,384]{1,0:T(8,128)}, f32[8,384,384]{2,1,0:T(8,128)}, f32[8,384]{1,0:T(8,128)}, /*index=5*/s32[]{:T(128)}, s32[]{:T(128)}) while((s32[]{:T(128)}, f32[384]{0:T(512)S(1)}, f32[8,384]{1,0:T(8,128)}, f32[8,384,384]{2,1,0:T(8,128)}, f32[8,384]{1,0:T(8,128)}, ...), condition=%wide.region_4.5_spmd.clone, body=%wide.region_3.4_spmd.clone.sunk | while | flops 1770243 | bytes 612971 | solution.py:55
  100.8 1.7 convolution_reduce_fusion.9
  102.5 0.7 dynamic-slice_reduce_fusion.2
  103.3 1.3 dynamic_update_slice.13
  104.6 1.7 convolution_reduce_fusion.9
  106.3 0.7 dynamic-slice_reduce_fusion.2
  107.1 1.3 dynamic_update_slice.13
  108.4 1.7 convolution_reduce_fusion.9
  110.1 0.7 dynamic-slice_reduce_fusion.2
  110.9 1.3 dynamic_update_slice.13
  112.2 1.7 convolution_reduce_fusion.9
  114.7 1.3 dynamic_update_slice.13
  116.0 1.7 convolution_reduce_fusion.9
  118.5 1.3 dynamic_update_slice.13
  119.8 1.7 convolution_reduce_fusion.9
  122.3 1.3 dynamic_update_slice.13
  123.6 1.7 convolution_reduce_fusion.9
  126.1 1.3 dynamic_update_slice.13
  127.5 1.7 convolution_reduce_fusion.9
  129.9 1.3 dynamic_update_slice.13
  132.0 2.1 collective-permute-start.5
  134.1 6.1 %collective-permute-done.5 = f32[384]{0:T(512)S(1)} collective-permute-done((f32[384]{0:T(512)S(1)}, f32[384]{0:T(512)S(1)}, u32[]{:S(2)}, u32[]{:S(2)}) %collective-permute-start.5) | collective-permute-done | bytes 1568 | tf_op jit(solution)/shard_map/ppermute | solution.py:10
  140.2 1.3 fusion.15
  141.5 2.9 %collective-permute-start.4 = (f32[384,384]{1,0:T(8,128)S(1)}, f32[384,384]{1,0:T(8,128)S(1)}, u32[]{:S(2)}, u32[]{:S(2)}) collective-permute-start(f32[384,384]{1,0:T(8,128)S(1)} %fusion.15), channel_id=1, source_target_pairs={{0,64},{4,68},{8,72},{12,76},{16,80},{20,84},{24,88},{28,92},{32,9... | collective-permute-start | bytes 1769480 | tf_op jit(solution)/shard_map/ppermute | solution.py:10
  145.1 1.9 collective-permute-start.6
  147.0 24.4 %collective-permute-done.6 = f32[384]{0:T(512)S(1)} collective-permute-done((f32[384]{0:T(512)S(1)}, f32[384]{0:T(512)S(1)}, u32[]{:S(2)}, u32[]{:S(2)}) %collective-permute-start.6) | collective-permute-done | bytes 1568 | tf_op jit(solution)/shard_map/ppermute | solution.py:10
  172.1 1.9 collective-permute-start.7
  174.0 7.2 %collective-permute-done.7 = f32[384]{0:T(512)S(1)} collective-permute-done((f32[384]{0:T(512)S(1)}, f32[384]{0:T(512)S(1)}, u32[]{:S(2)}, u32[]{:S(2)}) %collective-permute-start.7) | collective-permute-done | bytes 1568 | tf_op jit(solution)/shard_map/ppermute | solution.py:10
  181.8 1.9 collective-permute-start.8
  183.8 4.8 %collective-permute-done.8 = f32[384]{0:T(512)S(1)} collective-permute-done((f32[384]{0:T(512)S(1)}, f32[384]{0:T(512)S(1)}, u32[]{:S(2)}, u32[]{:S(2)}) %collective-permute-start.8) | collective-permute-done | bytes 1568 | tf_op jit(solution)/shard_map/ppermute | solution.py:10
  189.2 1.9 collective-permute-start.9
  191.1 5.7 %collective-permute-done.9 = f32[384]{0:T(512)S(1)} collective-permute-done((f32[384]{0:T(512)S(1)}, f32[384]{0:T(512)S(1)}, u32[]{:S(2)}, u32[]{:S(2)}) %collective-permute-start.9) | collective-permute-done | bytes 1568 | tf_op jit(solution)/shard_map/ppermute | solution.py:10
  197.5 1.3 collective-permute-start.10
  198.8 8.1 %collective-permute-done.10 = f32[384]{0:T(512)S(1)} collective-permute-done((f32[384]{0:T(512)S(1)}, f32[384]{0:T(512)S(1)}, u32[]{:S(2)}, u32[]{:S(2)}) %collective-permute-start.10) | collective-permute-done | bytes 1568 | tf_op jit(solution)/shard_map/ppermute | solution.py:10
  206.9 1.3 fusion.16
  208.8 1.9 collective-permute-start.11
  210.8 6.3 %collective-permute-done.11 = f32[384]{0:T(512)S(1)} collective-permute-done((f32[384]{0:T(512)S(1)}, f32[384]{0:T(512)S(1)}, u32[]{:S(2)}, u32[]{:S(2)}) %collective-permute-start.11) | collective-permute-done | bytes 1568 | tf_op jit(solution)/shard_map/ppermute | solution.py:10
  217.1 6.4 %fusion.18 = f32[1,8,384]{2,0,1:T(1,128)S(1)} fusion(f32[8,384,384]{2,1,0:T(8,128)} %get-tuple-element.54, f32[384,1,1]{0,1,2:T(1,128)S(1)} %reshape.75), kind=kOutput, calls=%fused_computation.42 | convolution fusion | flops 14155776 | bytes 4732416 | tf_op jit(solution)/shard_map/lsq,q->ls/dot_general | solution.py:74
  (110 shorter events, 12.8 us)
Async XLA Ops:
  0.0 80.9 %copy-start = (f32[8,384,48]{1,2,0:T(8,128)S(1)}, f32[8,384,48]{1,2,0:T(8,128)}, u32[]{:S(2)}) copy-start(f32[8,384,48]{1,2,0:T(8,128)} %param.12) | copy-start | bytes 1769476
  0.1 28.8 %copy-start.5 = (s32[512]{0:T(512)S(1)}, s32[512]{0:T(512)}, u32[]{:S(2)}) copy-start(s32[512]{0:T(512)} %param.16) | copy-start | bytes 6148
  0.1 28.9 %copy-start.1 = (bf16[512,192]{0,1:T(8,128)(2,1)S(1)}, bf16[512,192]{0,1:T(8,128)(2,1)}, u32[]{:S(2)}) copy-start(bf16[512,192]{0,1:T(8,128)(2,1)} %param.14) | copy-start | bytes 589828
  0.1 28.8 %copy-start.4 = (f32[512]{0:T(512)S(1)}, f32[512]{0:T(512)}, u32[]{:S(2)}) copy-start(f32[512]{0:T(512)} %param.15) | copy-start | bytes 6148
  0.1 44.5 %copy-start.6 = (s32[1,64]{1,0:T(1,128)S(1)}, s32[1,64]{1,0:T(1,128)}, u32[]{:S(2)}) copy-start(s32[1,64]{1,0:T(1,128)} %param.17) | copy-start | bytes 772
  25.8 36.0 %copy-start.3 = (f32[384]{0:T(512)S(1)}, f32[384]{0:T(512)}, u32[]{:S(2)}) copy-start(f32[384]{0:T(512)} %param.13) | copy-start | bytes 4612
  26.9 14.5 %collective-permute-start = (f32[384,384]{1,0:T(8,128)S(1)}, f32[384,384]{1,0:T(8,128)S(1)}, u32[]{:S(2)}, u32[]{:S(2)}) collective-permute-start(f32[384,384]{1,0:T(8,128)S(1)} %bitcast_select_fusion), channel_id=1, source_target_pairs={{0,4},{4,8},{8,12},{12,16},{16,20},{20,24},{24,28},{28,32},{32,36}... | collective-permute-start | bytes 1769480 | tf_op jit(solution)/shard_map/ppermute | solution.py:10
  42.7 30.2 %collective-permute-start.1 = (f32[384,384]{1,0:T(8,128)S(1)}, f32[384,384]{1,0:T(8,128)S(1)}, u32[]{:S(2)}, u32[]{:S(2)}) collective-permute-start(f32[384,384]{1,0:T(8,128)S(1)} %fusion.12), channel_id=1, source_target_pairs={{0,8},{4,12},{8,16},{12,20},{16,24},{20,28},{24,32},{28,36},{32,40... | collective-permute-start | bytes 1769480 | tf_op jit(solution)/shard_map/ppermute | solution.py:10
  47.8 24.3 %all-to-all-start = ((bf16[256,2,196]{2,1,0:T(2,128)(2,1)}), bf16[256,2,196]{2,1,0:T(2,128)(2,1)S(1)}, u32[]{:S(2)}, u32[]{:S(2)}) async-start(bf16[256,2,196]{2,1,0:T(2,128)(2,1)} %reshape.87), calls=%async_computation | async-start | bytes 524288 | tf_op jit(solution)/shard_map/all_to_all | solution.py:35
  74.2 22.8 %collective-permute-start.2 = (f32[384,384]{1,0:T(8,128)S(1)}, f32[384,384]{1,0:T(8,128)S(1)}, u32[]{:S(2)}, u32[]{:S(2)}) collective-permute-start(f32[384,384]{1,0:T(8,128)S(1)} %fusion.13), channel_id=1, source_target_pairs={{0,16},{4,20},{8,24},{12,28},{16,32},{20,36},{24,40},{28,44},{32,4... | collective-permute-start | bytes 1769480 | tf_op jit(solution)/shard_map/ppermute | solution.py:10
  98.2 42.0 %collective-permute-start.3 = (f32[384,384]{1,0:T(8,128)S(1)}, f32[384,384]{1,0:T(8,128)S(1)}, u32[]{:S(2)}, u32[]{:S(2)}) collective-permute-start(f32[384,384]{1,0:T(8,128)S(1)} %fusion.14), channel_id=1, source_target_pairs={{0,32},{4,36},{8,40},{12,44},{16,48},{20,52},{24,56},{28,60},{32,6... | collective-permute-start | bytes 1769480 | tf_op jit(solution)/shard_map/ppermute | solution.py:10
  132.0 8.2 %collective-permute-start.5 = (f32[384]{0:T(512)S(1)}, f32[384]{0:T(512)S(1)}, u32[]{:S(2)}, u32[]{:S(2)}) collective-permute-start(f32[384]{0:T(512)S(1)} %add_select_fusion), channel_id=1, source_target_pairs={{0,4},{4,8},{8,12},{12,16},{16,20},{20,24},{24,28},{28,32},{32,36}... | collective-permute-start | bytes 4616 | tf_op jit(solution)/shard_map/ppermute | solution.py:10
  141.5 65.4 %collective-permute-start.4 = (f32[384,384]{1,0:T(8,128)S(1)}, f32[384,384]{1,0:T(8,128)S(1)}, u32[]{:S(2)}, u32[]{:S(2)}) collective-permute-start(f32[384,384]{1,0:T(8,128)S(1)} %fusion.15), channel_id=1, source_target_pairs={{0,64},{4,68},{8,72},{12,76},{16,80},{20,84},{24,88},{28,92},{32,9... | collective-permute-start | bytes 1769480 | tf_op jit(solution)/shard_map/ppermute | solution.py:10
  145.1 26.3 %collective-permute-start.6 = (f32[384]{0:T(512)S(1)}, f32[384]{0:T(512)S(1)}, u32[]{:S(2)}, u32[]{:S(2)}) collective-permute-start(f32[384]{0:T(512)S(1)} %add.36), channel_id=1, source_target_pairs={{0,8},{4,12},{8,16},{12,20},{16,24},{20,28},{24,32},{28,36},{32,40... | collective-permute-start | bytes 4616 | tf_op jit(solution)/shard_map/ppermute | solution.py:10
  171.4 52.0 %copy-start.2 = (f32[8,384]{1,0:T(8,128)S(1)}, f32[8,384]{1,0:T(8,128)}, u32[]{:S(2)}) copy-start(f32[8,384]{1,0:T(8,128)} %get-tuple-element.55) | copy-start | bytes 36868
  172.1 9.1 %collective-permute-start.7 = (f32[384]{0:T(512)S(1)}, f32[384]{0:T(512)S(1)}, u32[]{:S(2)}, u32[]{:S(2)}) collective-permute-start(f32[384]{0:T(512)S(1)} %add.37), channel_id=1, source_target_pairs={{0,16},{4,20},{8,24},{12,28},{16,32},{20,36},{24,40},{28,44},{32,4... | collective-permute-start | bytes 4616 | tf_op jit(solution)/shard_map/ppermute | solution.py:10
  181.8 6.7 %collective-permute-start.8 = (f32[384]{0:T(512)S(1)}, f32[384]{0:T(512)S(1)}, u32[]{:S(2)}, u32[]{:S(2)}) collective-permute-start(f32[384]{0:T(512)S(1)} %add.38), channel_id=1, source_target_pairs={{0,32},{4,36},{8,40},{12,44},{16,48},{20,52},{24,56},{28,60},{32,6... | collective-permute-start | bytes 4616 | tf_op jit(solution)/shard_map/ppermute | solution.py:10
  189.2 7.6 %collective-permute-start.9 = (f32[384]{0:T(512)S(1)}, f32[384]{0:T(512)S(1)}, u32[]{:S(2)}, u32[]{:S(2)}) collective-permute-start(f32[384]{0:T(512)S(1)} %add.39), channel_id=1, source_target_pairs={{0,64},{4,68},{8,72},{12,76},{16,80},{20,84},{24,88},{28,92},{32,9... | collective-permute-start | bytes 4616 | tf_op jit(solution)/shard_map/ppermute | solution.py:10
  197.5 9.4 %collective-permute-start.10 = (f32[384]{0:T(512)S(1)}, f32[384]{0:T(512)S(1)}, u32[]{:S(2)}, u32[]{:S(2)}) collective-permute-start(f32[384]{0:T(512)S(1)} %add.40), channel_id=1, source_target_pairs={{0,128},{4,132},{8,136},{12,140},{16,144},{20,148},{24,152},{28,15... | collective-permute-start | bytes 4616 | tf_op jit(solution)/shard_map/ppermute | solution.py:10
  208.8 8.2 %collective-permute-start.11 = (f32[384]{0:T(512)S(1)}, f32[384]{0:T(512)S(1)}, u32[]{:S(2)}, u32[]{:S(2)}) collective-permute-start(f32[384]{0:T(512)S(1)} %add.41), channel_id=1, source_target_pairs={{0,4},{4,8},{8,12},{12,16},{16,20},{20,24},{24,28},{28,32},{32,36}... | collective-permute-start | bytes 4616 | tf_op jit(solution)/shard_map/ppermute | solution.py:10
where the time goes:
time: 226 us; the launch traced here: 224 us
  waiting for transfers between devices  83.5 us (37%)
  matrix products  59.6 us (26%)
  starting transfers between devices  39.5 us (17%)
  local copies, waits for them, and re-layouts  22.4 us (10%)
  blocking collectives  15.5 us (7%)
  other arithmetic  2.82 us (1%)
    ppermute x12, waiting for transfers between devices, passed_along(): return lax.ppermute(block, axis, route)  74.9 us
    ppermute x12, starting transfers between devices, passed_along(): return lax.ppermute(block, axis, route)  25.6 us
    dot_general x8, matrix products, compose(): prefix = jnp.dot(step_map, prefix, precision=exact)  25.3 us
    psum x1, blocking collectives, on_device(): forcing = lax.psum(partial_force, 'ingest')  15.5 us
    all_to_all x1, starting transfers between devices, on_device(): lax.all_to_all(sent, ('tm', 'ingest'), split_axis=0, concat_axis=0, tiled...  13.9 us
    dot_general x8, matrix products, advance(): offset = jnp.dot(step_map, offset, precision=exact) + step_force  13.8 us
    dynamic_update_slice x8, local copies, waits for them, and re-layouts, on_device(): lax.scan(advance, jnp.zeros((state_width,), jnp.float32), (trans, forcing))  10.6 us
    all_to_all x1, waiting for transfers between devices, on_device(): lax.all_to_all(sent, ('tm', 'ingest'), split_axis=0, concat_axis=0, tiled...  8.65 us
  transfers between devices with their start and end apart: 13, of which 9 were waited for; matrix products, arithmetic and copies ran while one was open for 20% of the time, Pallas kernels for 0%

commit v1 on v0

--- a/solution.py
+++ b/solution.py
@@ -39,7 +39,7 @@
     onehot = (got_marks[:, None] == step_ids).astype(jnp.bfloat16)
     drive_piece = jnp.einsum("rl,rq->lq", onehot, got_rows, preferred_element_type=jnp.float32)
     partial_force = jnp.einsum("lsq,lq->ls", gain, drive_piece, precision=exact)
-    forcing = lax.psum(partial_force, "ingest")
+    forcing = jnp.sum(lax.all_gather(partial_force, "ingest"), axis=0)
 
     def compose(prefix, step_map):
         prefix = jnp.dot(step_map, prefix, precision=exact)

time: 226 us -> 216 us (0.956)
  waiting for transfers between devices: 83.5 us -> 76.6 us
  blocking collectives: 15.5 us -> 12 us
    psum x1 -> x0, blocking collectives: 15.5 us -> none  [on_device(): forcing = lax.psum(partial_force, 'ingest')]
    all_gather x0 -> x1, blocking collectives: none -> 12 us  [on_device(): forcing = jnp.sum(lax.all_gather(partial_force, 'ingest'), axis=0)]
    all_to_all x1, waiting for transfers between devices: 8.65 us -> 4.14 us  [on_device(): lax.all_to_all(sent, ('tm', 'ingest'), split_axis=0, concat_axis=0, tiled...]
    ppermute x12, waiting for transfers between devices: 74.9 us -> 72.5 us  [passed_along(): return lax.ppermute(block, axis, route)]
  transfers between devices with their start and end apart: 13 -> 13, of which waited for: 9 -> 10; matrix products, arithmetic and copies ran while one was open for 20% -> 22% of each run, Pallas kernels for 0% -> 0%
where the time goes in v1:
time: 216 us; the launch traced here: 214 us
  waiting for transfers between devices  76.6 us (35%)
  matrix products  59.6 us (28%)
  starting transfers between devices  38.9 us (18%)
  local copies, waits for them, and re-layouts  22.4 us (10%)
  blocking collectives  12 us (6%)
  other arithmetic  3.42 us (2%)
    ppermute x12, waiting for transfers between devices, passed_along(): return lax.ppermute(block, axis, route)  72.5 us
    dot_general x8, matrix products, compose(): prefix = jnp.dot(step_map, prefix, precision=exact)  25.3 us
    ppermute x12, starting transfers between devices, passed_along(): return lax.ppermute(block, axis, route)  24.1 us
    all_to_all x1, starting transfers between devices, on_device(): lax.all_to_all(sent, ('tm', 'ingest'), split_axis=0, concat_axis=0, tiled...  14.8 us
    dot_general x8, matrix products, advance(): offset = jnp.dot(step_map, offset, precision=exact) + step_force  13.8 us
    all_gather x1, blocking collectives, on_device(): forcing = jnp.sum(lax.all_gather(partial_force, 'ingest'), axis=0)  12 us
    dynamic_update_slice x8, local copies, waits for them, and re-layouts, on_device(): lax.scan(advance, jnp.zeros((state_width,), jnp.float32), (trans, forcing))  10.6 us
    dot_general x1, matrix products, on_device(): jnp.einsum('lsq,q->ls', prefix_maps, entering, precision=exact) + offsets  6.36 us
  transfers between devices with their start and end apart: 13, of which 10 were waited for; matrix products, arithmetic and copies ran while one was open for 22% of the time, Pallas kernels for 0%

profile of v1, /device:TPU:128, one launch (start us, length us, event | category | flops | bytes accessed | tf_op | source)
XLA Modules:
  0.0 213.7 jit_solution(13174679708959057509)
XLA Ops:
  0.1 25.7 %while.25 = (s32[]{:T(128)}, f32[384,384]{1,0:T(8,128)S(1)}, f32[8,384,384]{2,1,0:T(8,128)}, f32[8,384,384]{2,1,0:T(8,128)}, s32[]{:T(128)}) while((s32[]{:T(128)}, f32[384,384]{1,0:T(8,128)S(1)}, f32[8,384,384]{2,1,0:T(8,128)}, f32[8,384,384]{2,1,0:T(8,128)}, s32[]{:T(128)}) %tuple.41), condition=%wide.region_1.2_spmd, body=%wide.region_0.1_spmd.sunk | while | flops 679477248 | bytes 3540037 | solution.py:48
  0.2 3.2 %bitcast_dynamic-update-slice_fusion.2 = (f32[8,384,384]{2,1,0:T(8,128)}, f32[384,384]{1,0:T(8,128)S(1)}) fusion(f32[8,384,384]{2,1,0:T(8,128)} %get-tuple-element.182, s32[]{:T(128)S(6)} %copy.46, f32[384,384]{1,0:T(8,128)S(1)} %copy.53, f32[8,384,384]{2,1,0:T(8,128)} %get-tuple-element.188), kind=kOutput, calls=%fused_computation.clone.1 | convolution fusion | flops 679477248 | bytes 2360320 | tf_op jit(solution)/shard_map/while/body/eval_jaxpr/dot_general | solution.py:45
  3.4 3.1 %bitcast_dynamic-update-slice_fusion.2 = (f32[8,384,384]{2,1,0:T(8,128)}, f32[384,384]{1,0:T(8,128)S(1)}) fusion(f32[8,384,384]{2,1,0:T(8,128)} %get-tuple-element.182, s32[]{:T(128)S(6)} %copy.46, f32[384,384]{1,0:T(8,128)S(1)} %copy.53, f32[8,384,384]{2,1,0:T(8,128)} %get-tuple-element.188), kind=kOutput, calls=%fused_computation.clone.1 | convolution fusion | flops 679477248 | bytes 2360320 | tf_op jit(solution)/shard_map/while/body/eval_jaxpr/dot_general | solution.py:45
  6.6 3.2 %bitcast_dynamic-update-slice_fusion.2 = (f32[8,384,384]{2,1,0:T(8,128)}, f32[384,384]{1,0:T(8,128)S(1)}) fusion(f32[8,384,384]{2,1,0:T(8,128)} %get-tuple-element.182, s32[]{:T(128)S(6)} %copy.46, f32[384,384]{1,0:T(8,128)S(1)} %copy.53, f32[8,384,384]{2,1,0:T(8,128)} %get-tuple-element.188), kind=kOutput, calls=%fused_computation.clone.1 | convolution fusion | flops 679477248 | bytes 2360320 | tf_op jit(solution)/shard_map/while/body/eval_jaxpr/dot_general | solution.py:45
  9.8 3.2 %bitcast_dynamic-update-slice_fusion.2 = (f32[8,384,384]{2,1,0:T(8,128)}, f32[384,384]{1,0:T(8,128)S(1)}) fusion(f32[8,384,384]{2,1,0:T(8,128)} %get-tuple-element.182, s32[]{:T(128)S(6)} %copy.46, f32[384,384]{1,0:T(8,128)S(1)} %copy.53, f32[8,384,384]{2,1,0:T(8,128)} %get-tuple-element.188), kind=kOutput, calls=%fused_computation.clone.1 | convolution fusion | flops 679477248 | bytes 2360320 | tf_op jit(solution)/shard_map/while/body/eval_jaxpr/dot_general | solution.py:45
  13.0 3.2 %bitcast_dynamic-update-slice_fusion.2 = (f32[8,384,384]{2,1,0:T(8,128)}, f32[384,384]{1,0:T(8,128)S(1)}) fusion(f32[8,384,384]{2,1,0:T(8,128)} %get-tuple-element.182, s32[]{:T(128)S(6)} %copy.46, f32[384,384]{1,0:T(8,128)S(1)} %copy.53, f32[8,384,384]{2,1,0:T(8,128)} %get-tuple-element.188), kind=kOutput, calls=%fused_computation.clone.1 | convolution fusion | flops 679477248 | bytes 2360320 | tf_op jit(solution)/shard_map/while/body/eval_jaxpr/dot_general | solution.py:45
  16.2 3.1 %bitcast_dynamic-update-slice_fusion.2 = (f32[8,384,384]{2,1,0:T(8,128)}, f32[384,384]{1,0:T(8,128)S(1)}) fusion(f32[8,384,384]{2,1,0:T(8,128)} %get-tuple-element.182, s32[]{:T(128)S(6)} %copy.46, f32[384,384]{1,0:T(8,128)S(1)} %copy.53, f32[8,384,384]{2,1,0:T(8,128)} %get-tuple-element.188), kind=kOutput, calls=%fused_computation.clone.1 | convolution fusion | flops 679477248 | bytes 2360320 | tf_op jit(solution)/shard_map/while/body/eval_jaxpr/dot_general | solution.py:45
  19.4 3.1 %bitcast_dynamic-update-slice_fusion.2 = (f32[8,384,384]{2,1,0:T(8,128)}, f32[384,384]{1,0:T(8,128)S(1)}) fusion(f32[8,384,384]{2,1,0:T(8,128)} %get-tuple-element.182, s32[]{:T(128)S(6)} %copy.46, f32[384,384]{1,0:T(8,128)S(1)} %copy.53, f32[8,384,384]{2,1,0:T(8,128)} %get-tuple-element.188), kind=kOutput, calls=%fused_computation.clone.1 | convolution fusion | flops 679477248 | bytes 2360320 | tf_op jit(solution)/shard_map/while/body/eval_jaxpr/dot_general | solution.py:45
  22.6 3.1 %bitcast_dynamic-update-slice_fusion.2 = (f32[8,384,384]{2,1,0:T(8,128)}, f32[384,384]{1,0:T(8,128)S(1)}) fusion(f32[8,384,384]{2,1,0:T(8,128)} %get-tuple-element.182, s32[]{:T(128)S(6)} %copy.46, f32[384,384]{1,0:T(8,128)S(1)} %copy.53, f32[8,384,384]{2,1,0:T(8,128)} %get-tuple-element.188), kind=kOutput, calls=%fused_computation.clone.1 | convolution fusion | flops 679477248 | bytes 2360320 | tf_op jit(solution)/shard_map/while/body/eval_jaxpr/dot_general | solution.py:45
  25.8 1.1 bitcast_select_fusion
  26.9 1.9 collective-permute-start
  30.6 0.8 reduce.20
  31.3 0.9 reshape.88
  32.2 14.8 %all-to-all-start = ((bf16[256,2,196]{2,1,0:T(2,128)(2,1)}), bf16[256,2,196]{2,1,0:T(2,128)(2,1)S(1)}, u32[]{:S(2)}, u32[]{:S(2)}) async-start(bf16[256,2,196]{2,1,0:T(2,128)(2,1)} %reshape.88), calls=%async_computation | async-start | bytes 524288 | tf_op jit(solution)/shard_map/all_to_all | solution.py:35
  47.1 1.3 fusion.12
  48.3 3.4 %collective-permute-start.1 = (f32[384,384]{1,0:T(8,128)S(1)}, f32[384,384]{1,0:T(8,128)S(1)}, u32[]{:S(2)}, u32[]{:S(2)}) collective-permute-start(f32[384,384]{1,0:T(8,128)S(1)} %fusion.12), channel_id=1, source_target_pairs={{0,8},{4,12},{8,16},{12,20},{16,24},{20,28},{24,32},{28,36},{32,40... | collective-permute-start | bytes 1769480 | tf_op jit(solution)/shard_map/ppermute | solution.py:10
  51.8 1.7 convolution_reduce_fusion.7
  53.5 4.1 %all-to-all-done = bf16[256,2,196]{2,1,0:T(2,128)(2,1)S(1)} async-done(((bf16[256,2,196]{2,1,0:T(2,128)(2,1)}), bf16[256,2,196]{2,1,0:T(2,128)(2,1)S(1)}, u32[]{:S(2)}, u32[]{:S(2)}) %all-to-all-start) | async-done | bytes 200736 | tf_op jit(solution)/shard_map/all_to_all | solution.py:35
  58.6 1.3 reshape.55
  60.1 9.0 %collective-permute-done.1 = f32[384,384]{1,0:T(8,128)S(1)} collective-permute-done((f32[384,384]{1,0:T(8,128)S(1)}, f32[384,384]{1,0:T(8,128)S(1)}, u32[]{:S(2)}, u32[]{:S(2)}) %collective-permute-start.1) | collective-permute-done | bytes 589856 | tf_op jit(solution)/shard_map/ppermute | solution.py:10
  69.1 1.3 fusion.13
  70.4 1.9 collective-permute-start.2
  72.3 1.7 fusion.7
  74.5 12.0 %all-gather = f32[32,384]{1,0:T(8,128)S(1)} all-gather(f32[8,384]{1,0:T(8,128)S(1)} %bitcast.76), channel_id=2, replica_groups=mesh['tm'=64,'ingest'=4] {'ingest'}, dimensions={0}, use_global_device_ids=true | all-gather | bytes 61440 | tf_op jit(solution)/shard_map/all_gather | solution.py:42
  87.2 3.2 %collective-permute-done.2 = f32[384,384]{1,0:T(8,128)S(1)} collective-permute-done((f32[384,384]{1,0:T(8,128)S(1)}, f32[384,384]{1,0:T(8,128)S(1)}, u32[]{:S(2)}, u32[]{:S(2)}) %collective-permute-start.2) | collective-permute-done | bytes 589856 | tf_op jit(solution)/shard_map/ppermute | solution.py:10
  90.3 1.3 fusion.14
  91.6 1.9 collective-permute-start.3
  93.5 30.5 %while.26 = (s32[]{:T(128)}, f32[384]{0:T(512)S(1)}, f32[8,384]{1,0:T(8,128)}, f32[8,384,384]{2,1,0:T(8,128)}, f32[8,384]{1,0:T(8,128)}, /*index=5*/s32[]{:T(128)}, s32[]{:T(128)}) while((s32[]{:T(128)}, f32[384]{0:T(512)S(1)}, f32[8,384]{1,0:T(8,128)}, f32[8,384,384]{2,1,0:T(8,128)}, f32[8,384]{1,0:T(8,128)}, ...), condition=%wide.region_4.5_spmd.clone, body=%wide.region_3.4_spmd.clone.sunk | while | flops 1770243 | bytes 612971 | solution.py:55
  93.6 1.7 convolution_reduce_fusion.9
  96.0 1.3 dynamic_update_slice.13
  97.4 1.7 convolution_reduce_fusion.9
  99.9 1.3 dynamic_update_slice.13
  101.2 1.7 convolution_reduce_fusion.9
  103.7 1.3 dynamic_update_slice.13
  105.0 1.7 convolution_reduce_fusion.9
  107.5 1.3 dynamic_update_slice.13
  108.8 1.7 convolution_reduce_fusion.9
  111.3 1.3 dynamic_update_slice.13
  112.6 1.7 convolution_reduce_fusion.9
  114.4 0.7 dynamic-slice_reduce_fusion.2
  115.1 1.3 dynamic_update_slice.13
  116.4 1.7 convolution_reduce_fusion.9
  118.2 0.7 dynamic-slice_reduce_fusion.2
  118.9 1.3 dynamic_update_slice.13
  120.3 1.7 convolution_reduce_fusion.9
  122.7 1.3 dynamic_update_slice.13
  124.8 2.1 collective-permute-start.5
  126.9 6.1 %collective-permute-done.5 = f32[384]{0:T(512)S(1)} collective-permute-done((f32[384]{0:T(512)S(1)}, f32[384]{0:T(512)S(1)}, u32[]{:S(2)}, u32[]{:S(2)}) %collective-permute-start.5) | collective-permute-done | bytes 1568 | tf_op jit(solution)/shard_map/ppermute | solution.py:10
  133.0 1.3 fusion.15
  134.3 1.9 collective-permute-start.4
  136.9 1.9 collective-permute-start.6
  138.8 22.2 %collective-permute-done.6 = f32[384]{0:T(512)S(1)} collective-permute-done((f32[384]{0:T(512)S(1)}, f32[384]{0:T(512)S(1)}, u32[]{:S(2)}, u32[]{:S(2)}) %collective-permute-start.6) | collective-permute-done | bytes 1568 | tf_op jit(solution)/shard_map/ppermute | solution.py:10
  161.7 1.9 collective-permute-start.7
  163.6 7.2 %collective-permute-done.7 = f32[384]{0:T(512)S(1)} collective-permute-done((f32[384]{0:T(512)S(1)}, f32[384]{0:T(512)S(1)}, u32[]{:S(2)}, u32[]{:S(2)}) %collective-permute-start.7) | collective-permute-done | bytes 1568 | tf_op jit(solution)/shard_map/ppermute | solution.py:10
  171.5 1.9 collective-permute-start.8
  173.4 4.8 %collective-permute-done.8 = f32[384]{0:T(512)S(1)} collective-permute-done((f32[384]{0:T(512)S(1)}, f32[384]{0:T(512)S(1)}, u32[]{:S(2)}, u32[]{:S(2)}) %collective-permute-start.8) | collective-permute-done | bytes 1568 | tf_op jit(solution)/shard_map/ppermute | solution.py:10
  178.8 1.9 collective-permute-start.9
  180.8 5.7 %collective-permute-done.9 = f32[384]{0:T(512)S(1)} collective-permute-done((f32[384]{0:T(512)S(1)}, f32[384]{0:T(512)S(1)}, u32[]{:S(2)}, u32[]{:S(2)}) %collective-permute-start.9) | collective-permute-done | bytes 1568 | tf_op jit(solution)/shard_map/ppermute | solution.py:10
  187.1 1.3 collective-permute-start.10
  188.4 8.1 %collective-permute-done.10 = f32[384]{0:T(512)S(1)} collective-permute-done((f32[384]{0:T(512)S(1)}, f32[384]{0:T(512)S(1)}, u32[]{:S(2)}, u32[]{:S(2)}) %collective-permute-start.10) | collective-permute-done | bytes 1568 | tf_op jit(solution)/shard_map/ppermute | solution.py:10
  196.5 1.3 fusion.16
  198.5 1.9 collective-permute-start.11
  200.4 6.3 %collective-permute-done.11 = f32[384]{0:T(512)S(1)} collective-permute-done((f32[384]{0:T(512)S(1)}, f32[384]{0:T(512)S(1)}, u32[]{:S(2)}, u32[]{:S(2)}) %collective-permute-start.11) | collective-permute-done | bytes 1568 | tf_op jit(solution)/shard_map/ppermute | solution.py:10
  206.7 6.4 %fusion.18 = f32[1,8,384]{2,0,1:T(1,128)S(1)} fusion(f32[8,384,384]{2,1,0:T(8,128)} %get-tuple-element.54, f32[384,1,1]{0,1,2:T(1,128)S(1)} %reshape.76), kind=kOutput, calls=%fused_computation.43 | convolution fusion | flops 14155776 | bytes 4732416 | tf_op jit(solution)/shard_map/lsq,q->ls/dot_general | solution.py:74
  (111 shorter events, 14.2 us)
Async XLA Ops:
  0.0 74.1 %copy-start = (f32[8,384,48]{1,2,0:T(8,128)S(1)}, f32[8,384,48]{1,2,0:T(8,128)}, u32[]{:S(2)}) copy-start(f32[8,384,48]{1,2,0:T(8,128)} %param.12) | copy-start | bytes 1769476
  0.1 28.8 %copy-start.5 = (s32[512]{0:T(512)S(1)}, s32[512]{0:T(512)}, u32[]{:S(2)}) copy-start(s32[512]{0:T(512)} %param.16) | copy-start | bytes 6148
  0.1 28.9 %copy-start.1 = (bf16[512,192]{0,1:T(8,128)(2,1)S(1)}, bf16[512,192]{0,1:T(8,128)(2,1)}, u32[]{:S(2)}) copy-start(bf16[512,192]{0,1:T(8,128)(2,1)} %param.14) | copy-start | bytes 589828
  0.1 28.8 %copy-start.4 = (f32[512]{0:T(512)S(1)}, f32[512]{0:T(512)}, u32[]{:S(2)}) copy-start(f32[512]{0:T(512)} %param.15) | copy-start | bytes 6148
  0.1 29.8 %copy-start.6 = (s32[1,64]{1,0:T(1,128)S(1)}, s32[1,64]{1,0:T(1,128)}, u32[]{:S(2)}) copy-start(s32[1,64]{1,0:T(1,128)} %param.17) | copy-start | bytes 772
  25.8 26.0 %copy-start.3 = (f32[384]{0:T(512)S(1)}, f32[384]{0:T(512)}, u32[]{:S(2)}) copy-start(f32[384]{0:T(512)} %param.13) | copy-start | bytes 4612
  26.9 20.2 %collective-permute-start = (f32[384,384]{1,0:T(8,128)S(1)}, f32[384,384]{1,0:T(8,128)S(1)}, u32[]{:S(2)}, u32[]{:S(2)}) collective-permute-start(f32[384,384]{1,0:T(8,128)S(1)} %bitcast_select_fusion), channel_id=1, source_target_pairs={{0,4},{4,8},{8,12},{12,16},{16,20},{20,24},{24,28},{28,32},{32,36}... | collective-permute-start | bytes 1769480 | tf_op jit(solution)/shard_map/ppermute | solution.py:10
  32.2 25.5 %all-to-all-start = ((bf16[256,2,196]{2,1,0:T(2,128)(2,1)}), bf16[256,2,196]{2,1,0:T(2,128)(2,1)S(1)}, u32[]{:S(2)}, u32[]{:S(2)}) async-start(bf16[256,2,196]{2,1,0:T(2,128)(2,1)} %reshape.88), calls=%async_computation | async-start | bytes 524288 | tf_op jit(solution)/shard_map/all_to_all | solution.py:35
  48.3 20.8 %collective-permute-start.1 = (f32[384,384]{1,0:T(8,128)S(1)}, f32[384,384]{1,0:T(8,128)S(1)}, u32[]{:S(2)}, u32[]{:S(2)}) collective-permute-start(f32[384,384]{1,0:T(8,128)S(1)} %fusion.12), channel_id=1, source_target_pairs={{0,8},{4,12},{8,16},{12,20},{16,24},{20,28},{24,32},{28,36},{32,40... | collective-permute-start | bytes 1769480 | tf_op jit(solution)/shard_map/ppermute | solution.py:10
  70.4 19.9 %collective-permute-start.2 = (f32[384,384]{1,0:T(8,128)S(1)}, f32[384,384]{1,0:T(8,128)S(1)}, u32[]{:S(2)}, u32[]{:S(2)}) collective-permute-start(f32[384,384]{1,0:T(8,128)S(1)} %fusion.13), channel_id=1, source_target_pairs={{0,16},{4,20},{8,24},{12,28},{16,32},{20,36},{24,40},{28,44},{32,4... | collective-permute-start | bytes 1769480 | tf_op jit(solution)/shard_map/ppermute | solution.py:10
  91.6 41.4 %collective-permute-start.3 = (f32[384,384]{1,0:T(8,128)S(1)}, f32[384,384]{1,0:T(8,128)S(1)}, u32[]{:S(2)}, u32[]{:S(2)}) collective-permute-start(f32[384,384]{1,0:T(8,128)S(1)} %fusion.14), channel_id=1, source_target_pairs={{0,32},{4,36},{8,40},{12,44},{16,48},{20,52},{24,56},{28,60},{32,6... | collective-permute-start | bytes 1769480 | tf_op jit(solution)/shard_map/ppermute | solution.py:10
  124.8 8.2 %collective-permute-start.5 = (f32[384]{0:T(512)S(1)}, f32[384]{0:T(512)S(1)}, u32[]{:S(2)}, u32[]{:S(2)}) collective-permute-start(f32[384]{0:T(512)S(1)} %add_select_fusion), channel_id=1, source_target_pairs={{0,4},{4,8},{8,12},{12,16},{16,20},{20,24},{24,28},{28,32},{32,36}... | collective-permute-start | bytes 4616 | tf_op jit(solution)/shard_map/ppermute | solution.py:10
  134.3 62.2 %collective-permute-start.4 = (f32[384,384]{1,0:T(8,128)S(1)}, f32[384,384]{1,0:T(8,128)S(1)}, u32[]{:S(2)}, u32[]{:S(2)}) collective-permute-start(f32[384,384]{1,0:T(8,128)S(1)} %fusion.15), channel_id=1, source_target_pairs={{0,64},{4,68},{8,72},{12,76},{16,80},{20,84},{24,88},{28,92},{32,9... | collective-permute-start | bytes 1769480 | tf_op jit(solution)/shard_map/ppermute | solution.py:10
  136.9 24.1 %collective-permute-start.6 = (f32[384]{0:T(512)S(1)}, f32[384]{0:T(512)S(1)}, u32[]{:S(2)}, u32[]{:S(2)}) collective-permute-start(f32[384]{0:T(512)S(1)} %add.34), channel_id=1, source_target_pairs={{0,8},{4,12},{8,16},{12,20},{16,24},{20,28},{24,32},{28,36},{32,40... | collective-permute-start | bytes 4616 | tf_op jit(solution)/shard_map/ppermute | solution.py:10
  161.0 52.0 %copy-start.2 = (f32[8,384]{1,0:T(8,128)S(1)}, f32[8,384]{1,0:T(8,128)}, u32[]{:S(2)}) copy-start(f32[8,384]{1,0:T(8,128)} %get-tuple-element.55) | copy-start | bytes 36868
  161.7 9.1 %collective-permute-start.7 = (f32[384]{0:T(512)S(1)}, f32[384]{0:T(512)S(1)}, u32[]{:S(2)}, u32[]{:S(2)}) collective-permute-start(f32[384]{0:T(512)S(1)} %add.35), channel_id=1, source_target_pairs={{0,16},{4,20},{8,24},{12,28},{16,32},{20,36},{24,40},{28,44},{32,4... | collective-permute-start | bytes 4616 | tf_op jit(solution)/shard_map/ppermute | solution.py:10
  171.5 6.7 %collective-permute-start.8 = (f32[384]{0:T(512)S(1)}, f32[384]{0:T(512)S(1)}, u32[]{:S(2)}, u32[]{:S(2)}) collective-permute-start(f32[384]{0:T(512)S(1)} %add.36), channel_id=1, source_target_pairs={{0,32},{4,36},{8,40},{12,44},{16,48},{20,52},{24,56},{28,60},{32,6... | collective-permute-start | bytes 4616 | tf_op jit(solution)/shard_map/ppermute | solution.py:10
  178.8 7.6 %collective-permute-start.9 = (f32[384]{0:T(512)S(1)}, f32[384]{0:T(512)S(1)}, u32[]{:S(2)}, u32[]{:S(2)}) collective-permute-start(f32[384]{0:T(512)S(1)} %add.37), channel_id=1, source_target_pairs={{0,64},{4,68},{8,72},{12,76},{16,80},{20,84},{24,88},{28,92},{32,9... | collective-permute-start | bytes 4616 | tf_op jit(solution)/shard_map/ppermute | solution.py:10
  187.1 9.4 %collective-permute-start.10 = (f32[384]{0:T(512)S(1)}, f32[384]{0:T(512)S(1)}, u32[]{:S(2)}, u32[]{:S(2)}) collective-permute-start(f32[384]{0:T(512)S(1)} %add.38), channel_id=1, source_target_pairs={{0,128},{4,132},{8,136},{12,140},{16,144},{20,148},{24,152},{28,15... | collective-permute-start | bytes 4616 | tf_op jit(solution)/shard_map/ppermute | solution.py:10
  198.5 8.2 %collective-permute-start.11 = (f32[384]{0:T(512)S(1)}, f32[384]{0:T(512)S(1)}, u32[]{:S(2)}, u32[]{:S(2)}) collective-permute-start(f32[384]{0:T(512)S(1)} %add.39), channel_id=1, source_target_pairs={{0,4},{4,8},{8,12},{12,16},{16,20},{20,24},{24,28},{28,32},{32,36}... | collective-permute-start | bytes 4616 | tf_op jit(solution)/shard_map/ppermute | solution.py:10
